TPU v7x, 32 devices: a whole 2x2x4 slice. The times are simulated.
32 devices in a mesh: parts: 2 (over x), seq: 16 (over z, y, core).
Axes of the slice: x: 2, y: 2, z: 4, core: 2. Of those that a mesh axis runs over, the one named last changes fastest.
Arguments:
- queries: bfloat16 [4096, 2048], P(('parts', 'seq')), parts along dimension 0
- joined_keys_values: bfloat16 [4096, 2048], P(('parts', 'seq')), parts along dimension 0
- segment_ids: int32 [4096], P(('parts', 'seq')), parts along dimension 0, may hold values from 0 to 3, never falling along the last dimension, each value on 1 to 1024 neighbouring positions
- residual: bfloat16 [4096, 2688], P(('parts', 'seq')), parts along dimension 0, may hold values from -4 to 4
- norm_gain: float32 [2688], replicated, may hold values from 0.5 to 1.5
- out_proj: bfloat16 [2048, 2688], P('seq'), may hold values from -1 to 1
- head_weight: bfloat16 [16384, 2688], P('seq')
- next_ids: int32 [128], P('parts'), parts along dimension 0, may hold values from 0 to 16383
Outputs:
- layer_out: bfloat16 [4096, 2688], P(('parts', 'seq')), parts along dimension 0
- log_probs: float32 [128, 16384], P('parts', 'seq'), parts along dimension 0
- target_logp: float32 [128], P(('parts', 'seq')), parts along dimension 0
There are 2 independent parts, one for each index of `parts`. A program takes and returns all parts, laid end to end along the dimension named above; an argument that names none is the same for every part. Nothing has to cross between parts.
All inputs are finite; a program needn't handle non-finite values.
Results may differ from a plain program's by a relative error of at most 0.0056.
Values may be sent and summed in bfloat16 or wider, within the bound.
No kernel may reach another device: no remote copies, remote signals or barrier semaphores. Data moves between devices by JAX's collectives and lax.ppermute only.
A program may use at most 64 MiB of HBM per device.

v0:
```python
import jax
import jax.numpy as jnp
from jax import lax
from jax.sharding import PartitionSpec as P

QUERY_HEADS = 16
KEY_VALUE_HEADS = 8
HEAD_SIZE = 128
ATTENTION_SPAN = 1024
SCORE_DEV = 4
score_scale = 168.0 ** (-0.5)
masked_score = -1e30


def shifted(value, axis, steps):
    count = lax.axis_size(axis)
    leading, last = (max(0, -steps), min(count, count - steps))
    return lax.ppermute(value, axis, [(source, source + steps) for source in range(leading, last)])


def normalize(hidden, norm_gain):
    mean_square = jnp.mean(hidden * hidden, axis=1, keepdims=True)
    return (hidden * lax.rsqrt(mean_square + 1e-06) * norm_gain[None, :]).astype(jnp.bfloat16)


def local(
    queries, joined_keys_values, segment_ids, residual, norm_gain, out_proj, head_weight, next_ids
):
    token_rows = queries.shape[0]
    blocks = ATTENTION_SPAN // token_rows
    queries_per_group = QUERY_HEADS // KEY_VALUE_HEADS
    my_index = lax.axis_index("seq")
    first_row = my_index * token_rows
    rim_kv_parts = []
    rim_seg_parts = []
    for distance in range(blocks, 0, -1):
        moved_kv, moved_seg = shifted((joined_keys_values, segment_ids), "seq", distance)
        rim_kv_parts.append(moved_kv)
        rim_seg_parts.append(moved_seg)
    rim_kv = jnp.concatenate(rim_kv_parts, 0)
    rim_seg = jnp.concatenate(rim_seg_parts, 0)
    key_value_pair = jnp.concatenate([rim_kv, joined_keys_values], 0)
    key_seg = jnp.concatenate([rim_seg, segment_ids], 0)
    count_of_keys = key_value_pair.shape[0]
    query_pos = first_row + jnp.arange(token_rows, dtype=jnp.int32)
    key_pos = first_row - blocks * token_rows + jnp.arange(count_of_keys, dtype=jnp.int32)
    allowed = (segment_ids[:, None] == key_seg[None, :]) & (key_pos[None, :] >= 0)
    allowed = (
        allowed
        & (key_pos[None, :] <= query_pos[:, None])
        & (key_pos[None, :] > query_pos[:, None] - ATTENTION_SPAN)
    )
    heads_for_queries = queries.reshape(token_rows, KEY_VALUE_HEADS, queries_per_group, HEAD_SIZE)
    heads_for_keys = key_value_pair[:, : KEY_VALUE_HEADS * HEAD_SIZE].reshape(
        count_of_keys, KEY_VALUE_HEADS, HEAD_SIZE
    )
    heads_for_values = key_value_pair[:, KEY_VALUE_HEADS * HEAD_SIZE :].reshape(
        count_of_keys, KEY_VALUE_HEADS, HEAD_SIZE
    )
    scores = (
        jnp.einsum(
            "qhgd,khd->hgqk", heads_for_queries, heads_for_keys, preferred_element_type=jnp.float32
        )
        * score_scale
    )
    scores = jnp.where(allowed[None, None, :, :], scores, masked_score)
    row_max = jnp.max(scores, axis=-1, keepdims=True)
    raised = jnp.exp(scores - row_max)
    weights = (raised / jnp.sum(raised, axis=-1, keepdims=True)).astype(jnp.bfloat16)
    context = jnp.einsum(
        "hgqk,khd->qhgd", weights, heads_for_values, preferred_element_type=jnp.float32
    )
    context = context.reshape(token_rows, QUERY_HEADS * HEAD_SIZE).astype(jnp.bfloat16)
    width = residual.shape[1]
    projected = jnp.dot(
        context,
        lax.all_gather(out_proj, "seq", axis=0, tiled=True),
        preferred_element_type=jnp.float32,
    )
    hidden = residual.astype(jnp.float32) + projected
    layer_out = hidden.astype(jnp.bfloat16)
    score_count = SCORE_DEV
    stride = token_rows // score_count
    picked = hidden.reshape(score_count, stride, width)[:, stride - 1, :]
    normed = normalize(picked, norm_gain)
    logits = lax.dot_general(
        lax.all_gather(normed, "seq", axis=0, tiled=True),
        head_weight,
        (((1,), (1,)), ((), ())),
        preferred_element_type=jnp.float32,
    )
    global_max = lax.pmax(jnp.max(logits, axis=1), "seq")
    global_total = lax.psum(jnp.sum(jnp.exp(logits - global_max[:, None]), axis=1), "seq")
    log_total = global_max + jnp.log(global_total)
    log_probs = logits - log_total[:, None]
    vocab_width = head_weight.shape[0]
    local_ids = next_ids - my_index * vocab_width
    vocab_ids = jnp.arange(vocab_width, dtype=jnp.int32)
    picked_terms = jnp.sum(
        jnp.where(local_ids[:, None] == vocab_ids[None, :], log_probs, 0.0), axis=1
    )
    target_logp = lax.psum_scatter(picked_terms, "seq", scatter_dimension=0, tiled=True)
    return (layer_out, log_probs, target_logp)


def solution(mesh):
    in_specs = (
        P(("parts", "seq"), None),
        P(("parts", "seq"), None),
        P(("parts", "seq")),
        P(("parts", "seq"), None),
        P(),
        P("seq", None),
        P("seq", None),
        P("parts"),
    )
    out_specs = (P(("parts", "seq"), None), P("parts", "seq"), P(("parts", "seq")))
    return jax.shard_map(local, mesh=mesh, in_specs=in_specs, out_specs=out_specs, check_vma=False)
```

profile of v0, /device:TPU:0, one launch (start us, length us, event | category | flops | bytes accessed | tf_op | source)
XLA Modules:
  0.0 391.8 jit_solution(2573217400198368961)
XLA Ops:
  9.2 6.0 %collective-permute-start = (bf16[128,2048]{0,1:T(8,128)(2,1)S(1)}, bf16[128,2048]{0,1:T(8,128)(2,1)S(1)}, u32[]{:S(2)}, u32[]{:S(2)}) collective-permute-start(bf16[128,2048]{0,1:T(8,128)(2,1)S(1)} %copy.26), channel_id=1, source_target_pairs={{0,8},{1,9},{2,10},{3,11},{4,12},{5,13},{6,14},{7,15},{16,24},{17,... | collective-permute-start | bytes 1572872 | tf_op jit(solution)/shard_map/ppermute | solution.py:18
  15.2 3.6 collective-permute-start.1
  18.8 2.2 collective-permute-start.2
  22.3 1.9 collective-permute-start.8
  25.4 1.4 reshape.150
  28.8 53.5 %collective-permute-done.8 = s32[128]{0:T(128)S(1)} collective-permute-done((s32[128]{0:T(128)}, s32[128]{0:T(128)S(1)}, u32[]{:S(2)}, u32[]{:S(2)}) %collective-permute-start.8) | collective-permute-done | bytes 544 | tf_op jit(solution)/shard_map/ppermute | solution.py:18
  82.2 87.8 %collective-permute-start.9 = (s32[128]{0:T(128)}, s32[128]{0:T(128)S(1)}, u32[]{:S(2)}, u32[]{:S(2)}) collective-permute-start(s32[128]{0:T(128)} %param.10), channel_id=1, source_target_pairs={{0,7},{1,8},{2,9},{3,10},{4,11},{5,12},{6,13},{7,14},{8,15},{16,23... | collective-permute-start | bytes 1544 | tf_op jit(solution)/shard_map/ppermute | solution.py:18
  170.1 1.4 collective-permute-done.9
  171.5 1.7 collective-permute-start.10
  173.2 1.4 collective-permute-done.10
  177.3 8.0 %collective-permute-start.12 = (s32[128]{0:T(128)}, s32[128]{0:T(128)S(1)}, u32[]{:S(2)}, u32[]{:S(2)}) collective-permute-start(s32[128]{0:T(128)} %param.10), channel_id=1, source_target_pairs={{0,4},{1,5},{2,6},{3,7},{4,8},{5,9},{6,10},{7,11},{8,12},{9,13},{1... | collective-permute-start | bytes 1544 | tf_op jit(solution)/shard_map/ppermute | solution.py:18
  185.3 1.4 collective-permute-done.12
  186.7 3.1 collective-permute-start.13
  191.2 5.1 %collective-permute-start.14 = (s32[128]{0:T(128)}, s32[128]{0:T(128)S(1)}, u32[]{:S(2)}, u32[]{:S(2)}) collective-permute-start(s32[128]{0:T(128)} %param.10), channel_id=1, source_target_pairs={{0,2},{1,3},{2,4},{3,5},{4,6},{5,7},{6,8},{7,9},{8,10},{9,11},{10,... | collective-permute-start | bytes 1544 | tf_op jit(solution)/shard_map/ppermute | solution.py:18
  196.4 1.4 collective-permute-done.14
  197.8 1.6 collective-permute-start.15
  200.4 11.4 %collective-permute-start.4 = (bf16[128,2048]{0,1:T(8,128)(2,1)S(1)}, bf16[128,2048]{0,1:T(8,128)(2,1)S(1)}, u32[]{:S(2)}, u32[]{:S(2)}) collective-permute-start(bf16[128,2048]{0,1:T(8,128)(2,1)S(1)} %copy.26), channel_id=1, source_target_pairs={{0,4},{1,5},{2,6},{3,7},{4,8},{5,9},{6,10},{7,11},{8,12},{9,13},{1... | collective-permute-start | bytes 1572872 | tf_op jit(solution)/shard_map/ppermute | solution.py:18
  212.5 1.7 compare_and_fusion
  214.2 1.9 collective-permute-start.5
  216.3 2.2 collective-permute-start.6
  218.6 3.6 collective-permute-start.7
  222.6 2.7 collective-permute-done.5
  225.4 11.1 %collective-permute-done.6 = bf16[128,2048]{0,1:T(8,128)(2,1)S(1)} collective-permute-done((bf16[128,2048]{0,1:T(8,128)(2,1)S(1)}, bf16[128,2048]{0,1:T(8,128)(2,1)S(1)}, u32[]{:S(2)}, u32[]{:S(2)}) %collective-permute-start.6) | collective-permute-done | bytes 524320 | tf_op jit(solution)/shard_map/ppermute | solution.py:18
  236.9 1.8 fusion.27
  238.7 4.2 %fusion.28 = f32[8,2,128]{2,1,0:T(2,128)} fusion(pred[128,1152]{0,1:T(8,128)(4,1)S(1)} %compare_and_fusion, bf16[1152,8,128,1]{0,2,3,1:T(8,128)(2,1)S(1)} %bitcast.43, bf16[128,8,2,128]{3,2,1,0:T(2,128)(2,1)S(1)} %reshape.150), kind=kOutput, calls=%fused_computation.55 | convolution fusion | flops 613418112 | bytes 3039232 | tf_op jit(solution)/shard_map/sub | solution.py:68
  243.0 6.3 %fusion.6 = bf16[8,128,2,128]{3,1,2,0:T(8,128)(2,1)S(1)} fusion(bf16[1152,8,128,1]{0,2,3,1:T(8,128)(2,1)} %bitcast.45, f32[8,2,128]{2,1,0:T(2,128)} %fusion.28, pred[128,1152]{0,1:T(8,128)(4,1)S(1)} %compare_and_fusion, bf16[1152,8,128,1]{0,2,3,1:T(8,128)(2,1)S(1)} %bitcast.44, bf16[128,8,2,128]{3,2,1,0:T(2,128)(2,1)S(1)} %reshape.150), kind=kOutput, calls=%fused_computation.10 | convolution fusion | flops 1220021376 | bytes 5922816 | tf_op jit(solution)/shard_map/hgqk,khd->qhgd/dot_general | solution.py:70
  249.3 6.8 %fusion.31 = (bf16[128,2688]{1,0:T(8,128)(2,1)}, f32[128,2688]{1,0:T(8,128)S(1)}) fusion(bf16[128,2048]{0,1:T(8,128)(2,1)S(1)} %bitcast.47, bf16[2048,2688]{1,0:T(8,128)(2,1)} %all-gather.3.cloned.1.call-done, bf16[128,2688]{1,0:T(8,128)(2,1)} %param.11), kind=kOutput, calls=%fused_computation.56 | convolution fusion | flops 1410318336 | bytes 14286848 | tf_op jit(solution)/shard_map/dot_general | solution.py:75
  256.4 31.9 %all-gather = bf16[16,4,2688]{2,1,0:T(4,128)(2,1)S(1)} all-gather(bf16[1,4,2688]{2,1,0:T(4,128)(2,1)S(1)} %fusion.19), channel_id=1, replica_groups=mesh['parts'=2,'seq'=16] {'seq'}, dimensions={0}, use_global_device_ids=true | all-gather | bytes 365568 | tf_op jit(solution)/shard_map/all_gather | solution.py:87
  288.4 4.4 %fusion.32 = (f32[64]{0:T(128)S(1)}, f32[64,1024]{1,0:T(8,128)S(1)}) fusion(bf16[64,2688]{1,0:T(8,128)(2,1)S(1)} %reshape.153, bf16[1024,2688]{1,0:T(8,128)(2,1)} %param.14), kind=kOutput, calls=%fused_computation.57 | convolution fusion | flops 352387008 | bytes 6111488 | tf_op jit(solution)/shard_map/dot_general | solution.py:86
  292.9 31.4 %pmax.7 = f32[64]{0:T(128)S(1)} all-reduce(f32[64]{0:T(128)S(1)} %get-tuple-element.9), channel_id=1, replica_groups=mesh['parts'=2,'seq'=16] {'seq'}, use_global_device_ids=true, to_apply=%region_4.5 | all-reduce | flops 64 | bytes 512 | tf_op jit(solution)/shard_map/pmax | solution.py:92
  324.5 29.5 %psum.7 = f32[64]{0:T(128)S(1)} all-reduce(f32[64]{0:T(128)S(1)} %exponential_reduce_fusion), channel_id=1, replica_groups=mesh['parts'=2,'seq'=16] {'seq'}, use_global_device_ids=true, to_apply=%region_6.7 | all-reduce | flops 64 | bytes 512 | tf_op jit(solution)/shard_map/psum | solution.py:93
  354.9 29.5 %all-reduce = f32[64]{0:T(128)S(1)} all-reduce(f32[64]{0:T(128)S(1)} %get-tuple-element.3), channel_id=2, replica_groups=mesh['parts'=2,'seq'=16] {'seq'}, use_global_device_ids=true, to_apply=%region_8.9.clone | all-reduce | flops 64 | bytes 512
  (52 shorter events, 14.7 us)
Async XLA Ops:
  7.2 242.2 %all-gather.3.cloned.1.call-start = ((), (), s32[]{:S(2)}) async-start(), calls=%async_computation | async-start | bytes 11698176 | tf_op jit(solution)/shard_map/all_gather | solution.py:77
  9.2 205.0 %collective-permute-start = (bf16[128,2048]{0,1:T(8,128)(2,1)S(1)}, bf16[128,2048]{0,1:T(8,128)(2,1)S(1)}, u32[]{:S(2)}, u32[]{:S(2)}) collective-permute-start(bf16[128,2048]{0,1:T(8,128)(2,1)S(1)} %copy.26), channel_id=1, source_target_pairs={{0,8},{1,9},{2,10},{3,11},{4,12},{5,13},{6,14},{7,15},{16,24},{17,... | collective-permute-start | bytes 1572872 | tf_op jit(solution)/shard_map/ppermute | solution.py:18
  15.2 201.0 %collective-permute-start.1 = (bf16[128,2048]{0,1:T(8,128)(2,1)S(1)}, bf16[128,2048]{0,1:T(8,128)(2,1)S(1)}, u32[]{:S(2)}, u32[]{:S(2)}) collective-permute-start(bf16[128,2048]{0,1:T(8,128)(2,1)S(1)} %copy.26), channel_id=1, source_target_pairs={{0,7},{1,8},{2,9},{3,10},{4,11},{5,12},{6,13},{7,14},{8,15},{16,23... | collective-permute-start | bytes 1572872 | tf_op jit(solution)/shard_map/ppermute | solution.py:18
  18.8 199.8 %collective-permute-start.2 = (bf16[128,2048]{0,1:T(8,128)(2,1)S(1)}, bf16[128,2048]{0,1:T(8,128)(2,1)S(1)}, u32[]{:S(2)}, u32[]{:S(2)}) collective-permute-start(bf16[128,2048]{0,1:T(8,128)(2,1)S(1)} %copy.26), channel_id=1, source_target_pairs={{0,6},{1,7},{2,8},{3,9},{4,10},{5,11},{6,12},{7,13},{8,14},{9,15},... | collective-permute-start | bytes 1572872 | tf_op jit(solution)/shard_map/ppermute | solution.py:18
  21.0 201.3 %collective-permute-start.3 = (bf16[128,2048]{0,1:T(8,128)(2,1)S(1)}, bf16[128,2048]{0,1:T(8,128)(2,1)S(1)}, u32[]{:S(2)}, u32[]{:S(2)}) collective-permute-start(bf16[128,2048]{0,1:T(8,128)(2,1)S(1)} %copy.26), channel_id=1, source_target_pairs={{0,5},{1,6},{2,7},{3,8},{4,9},{5,10},{6,11},{7,12},{8,13},{9,14},{... | collective-permute-start | bytes 1572872 | tf_op jit(solution)/shard_map/ppermute | solution.py:18
  22.3 59.9 %collective-permute-start.8 = (s32[128]{0:T(128)}, s32[128]{0:T(128)S(1)}, u32[]{:S(2)}, u32[]{:S(2)}) collective-permute-start(s32[128]{0:T(128)} %param.10), channel_id=1, source_target_pairs={{0,8},{1,9},{2,10},{3,11},{4,12},{5,13},{6,14},{7,15},{16,24},{17,... | collective-permute-start | bytes 1544 | tf_op jit(solution)/shard_map/ppermute | solution.py:18
  82.2 89.3 %collective-permute-start.9 = (s32[128]{0:T(128)}, s32[128]{0:T(128)S(1)}, u32[]{:S(2)}, u32[]{:S(2)}) collective-permute-start(s32[128]{0:T(128)} %param.10), channel_id=1, source_target_pairs={{0,7},{1,8},{2,9},{3,10},{4,11},{5,12},{6,13},{7,14},{8,15},{16,23... | collective-permute-start | bytes 1544 | tf_op jit(solution)/shard_map/ppermute | solution.py:18
  171.5 3.1 collective-permute-start.10
  174.6 2.7 collective-permute-start.11
  177.3 9.5 %collective-permute-start.12 = (s32[128]{0:T(128)}, s32[128]{0:T(128)S(1)}, u32[]{:S(2)}, u32[]{:S(2)}) collective-permute-start(s32[128]{0:T(128)} %param.10), channel_id=1, source_target_pairs={{0,4},{1,5},{2,6},{3,7},{4,8},{5,9},{6,10},{7,11},{8,12},{9,13},{1... | collective-permute-start | bytes 1544 | tf_op jit(solution)/shard_map/ppermute | solution.py:18
  186.7 4.5 %collective-permute-start.13 = (s32[128]{0:T(128)}, s32[128]{0:T(128)S(1)}, u32[]{:S(2)}, u32[]{:S(2)}) collective-permute-start(s32[128]{0:T(128)} %param.10), channel_id=1, source_target_pairs={{0,3},{1,4},{2,5},{3,6},{4,7},{5,8},{6,9},{7,10},{8,11},{9,12},{10... | collective-permute-start | bytes 1544 | tf_op jit(solution)/shard_map/ppermute | solution.py:18
  191.2 6.6 %collective-permute-start.14 = (s32[128]{0:T(128)}, s32[128]{0:T(128)S(1)}, u32[]{:S(2)}, u32[]{:S(2)}) collective-permute-start(s32[128]{0:T(128)} %param.10), channel_id=1, source_target_pairs={{0,2},{1,3},{2,4},{3,5},{4,6},{5,7},{6,8},{7,9},{8,10},{9,11},{10,... | collective-permute-start | bytes 1544 | tf_op jit(solution)/shard_map/ppermute | solution.py:18
  197.8 2.6 collective-permute-start.15
  200.4 22.1 %collective-permute-start.4 = (bf16[128,2048]{0,1:T(8,128)(2,1)S(1)}, bf16[128,2048]{0,1:T(8,128)(2,1)S(1)}, u32[]{:S(2)}, u32[]{:S(2)}) collective-permute-start(bf16[128,2048]{0,1:T(8,128)(2,1)S(1)} %copy.26), channel_id=1, source_target_pairs={{0,4},{1,5},{2,6},{3,7},{4,8},{5,9},{6,10},{7,11},{8,12},{9,13},{1... | collective-permute-start | bytes 1572872 | tf_op jit(solution)/shard_map/ppermute | solution.py:18
  214.2 11.1 %collective-permute-start.5 = (bf16[128,2048]{0,1:T(8,128)(2,1)S(1)}, bf16[128,2048]{0,1:T(8,128)(2,1)S(1)}, u32[]{:S(2)}, u32[]{:S(2)}) collective-permute-start(bf16[128,2048]{0,1:T(8,128)(2,1)S(1)} %copy.26), channel_id=1, source_target_pairs={{0,3},{1,4},{2,5},{3,6},{4,7},{5,8},{6,9},{7,10},{8,11},{9,12},{10... | collective-permute-start | bytes 1572872 | tf_op jit(solution)/shard_map/ppermute | solution.py:18
  216.3 20.2 %collective-permute-start.6 = (bf16[128,2048]{0,1:T(8,128)(2,1)S(1)}, bf16[128,2048]{0,1:T(8,128)(2,1)S(1)}, u32[]{:S(2)}, u32[]{:S(2)}) collective-permute-start(bf16[128,2048]{0,1:T(8,128)(2,1)S(1)} %copy.26), channel_id=1, source_target_pairs={{0,2},{1,3},{2,4},{3,5},{4,6},{5,7},{6,8},{7,9},{8,10},{9,11},{10,... | collective-permute-start | bytes 1572872 | tf_op jit(solution)/shard_map/ppermute | solution.py:18
  218.6 18.0 %collective-permute-start.7 = (bf16[128,2048]{0,1:T(8,128)(2,1)S(1)}, bf16[128,2048]{0,1:T(8,128)(2,1)S(1)}, u32[]{:S(2)}, u32[]{:S(2)}) collective-permute-start(bf16[128,2048]{0,1:T(8,128)(2,1)S(1)} %copy.26), channel_id=1, source_target_pairs={{0,1},{1,2},{2,3},{3,4},{4,5},{5,6},{6,7},{7,8},{8,9},{9,10},{10,1... | collective-permute-start | bytes 1572872 | tf_op jit(solution)/shard_map/ppermute | solution.py:18
  249.3 7.0 %copy-start = (f32[2688]{0:T(1024)S(1)}, f32[2688]{0:T(1024)}, u32[]{:S(2)}) copy-start(f32[2688]{0:T(1024)} %param.12) | copy-start | bytes 32260
  256.1 97.9 %copy-start.1 = (s32[64]{0:T(128)S(1)}, s32[64]{0:T(128)}, u32[]{:S(2)}) copy-start(s32[64]{0:T(128)} %broadcast_subtract_fusion.1) | copy-start | bytes 772
Sparse Core Ops, SparseCore 0:
  10.3 136.2 all-gather.2
where the time goes:
time: 393 us; the launch traced here: 392 us
  starting transfers between devices  143 us (36%)
  blocking collectives  122 us (31%)
  waiting for transfers between devices  77.3 us (20%)
  matrix products  21.8 us (6%)
  between operations  15.1 us (4%)
  local copies, waits for them, and re-layouts  8.31 us (2%)
  other arithmetic  4.24 us (1%)
    ppermute x16, starting transfers between devices, shifted(): lax.ppermute(value, axis, [(source, source + steps) for source in range(l...  143 us
    ppermute x16, waiting for transfers between devices, shifted(): lax.ppermute(value, axis, [(source, source + steps) for source in range(l...  76.6 us
    all_gather x1, blocking collectives, local(): lax.all_gather(normed, 'seq', axis=0, tiled=True)  31.9 us
    pmax x1, blocking collectives, local(): global_max = lax.pmax(jnp.max(logits, axis=1), 'seq')  31.4 us
    unnamed x1, blocking collectives  29.5 us
    psum x1, blocking collectives, local(): lax.psum(jnp.sum(jnp.exp(logits - global_max[:, None]), axis=1), 'seq')  29.5 us
  transfers between devices with their start and end apart: 17, of which 10 were waited for; matrix products, arithmetic and copies ran while one was open for 5% of the time, Pallas kernels for 0%

commit v1 on v0

--- a/solution.py
+++ b/solution.py
@@ -10,6 +10,19 @@
 SCORE_DEV = 4
 score_scale = 168.0 ** (-0.5)
 masked_score = -1e30
+
+
+def ring_gather(array, axis, dim):
+    ways = lax.axis_size(axis)
+    up = [(d, (d + 1) % ways) for d in range(ways)]
+    down = [(d, (d - 1) % ways) for d in range(ways)]
+    earlier, later = ([array], [array])
+    for _ in range(ways // 2):
+        earlier.append(lax.ppermute(earlier[-1], axis, up))
+    for _ in range((ways - 1) // 2):
+        later.append(lax.ppermute(later[-1], axis, down))
+    line = jnp.concatenate([*earlier[::-1], *later[1:]], axis=dim)
+    return jnp.roll(line, (lax.axis_index(axis) - ways // 2) * array.shape[dim], axis=dim)
 
 
 def shifted(value, axis, steps):
@@ -84,7 +97,7 @@
     picked = hidden.reshape(score_count, stride, width)[:, stride - 1, :]
     normed = normalize(picked, norm_gain)
     logits = lax.dot_general(
-        lax.all_gather(normed, "seq", axis=0, tiled=True),
+        ring_gather(normed, "seq", 0),
         head_weight,
         (((1,), (1,)), ((), ())),
         preferred_element_type=jnp.float32,

time: 393 us -> 407 us (1.036)
  starting transfers between devices: 143 us -> 177 us
  blocking collectives: 122 us -> 88.5 us
  waiting for transfers between devices: 77.3 us -> 92.5 us
    ppermute x0 -> x15, starting transfers between devices: none -> 34.3 us  [the longest x8 18.4 us: ring_gather(): earlier.append(lax.ppermute(earlier[-1], axis, up))]
    all_gather x1 -> x0, blocking collectives: 31.9 us -> none  [local(): lax.all_gather(normed, 'seq', axis=0, tiled=True)]
    ppermute x0 -> x15, waiting for transfers between devices: none -> 12.1 us  [the longest x8 7.81 us: ring_gather(): earlier.append(lax.ppermute(earlier[-1], axis, up))]
  transfers between devices with their start and end apart: 17 -> 32, of which waited for: 10 -> 24; matrix products, arithmetic and copies ran while one was open for 5% -> 5% of each run, Pallas kernels for 0% -> 0%
where the time goes in v1:
time: 407 us; the launch traced here: 406 us
  starting transfers between devices  177 us (43%)
  waiting for transfers between devices  92.5 us (23%)
  blocking collectives  88.5 us (22%)
  matrix products  21.8 us (5%)
  between operations  15.2 us (4%)
  local copies, waits for them, and re-layouts  8.39 us (2%)
    ppermute x16, starting transfers between devices, shifted(): lax.ppermute(value, axis, [(source, source + steps) for source in range(l...  143 us
    ppermute x16, waiting for transfers between devices, shifted(): lax.ppermute(value, axis, [(source, source + steps) for source in range(l...  79.7 us
    pmax x1, blocking collectives, local(): global_max = lax.pmax(jnp.max(logits, axis=1), 'seq')  29.5 us
    unnamed x1, blocking collectives  29.5 us
    psum x1, blocking collectives, local(): lax.psum(jnp.sum(jnp.exp(logits - global_max[:, None]), axis=1), 'seq')  29.5 us
    ppermute x8, starting transfers between devices, ring_gather(): earlier.append(lax.ppermute(earlier[-1], axis, up))  18.4 us
    ppermute x7, starting transfers between devices, ring_gather(): later.append(lax.ppermute(later[-1], axis, down))  15.9 us
  transfers between devices with their start and end apart: 32, of which 24 were waited for; matrix products, arithmetic and copies ran while one was open for 5% of the time, Pallas kernels for 0%

profile of v1, /device:TPU:0, one launch (start us, length us, event | category | flops | bytes accessed | tf_op | source)
XLA Modules:
  0.0 406.4 jit_solution(11620603959413777650)
XLA Ops:
  9.2 6.0 %collective-permute-start = (bf16[128,2048]{0,1:T(8,128)(2,1)S(1)}, bf16[128,2048]{0,1:T(8,128)(2,1)S(1)}, u32[]{:S(2)}, u32[]{:S(2)}) collective-permute-start(bf16[128,2048]{0,1:T(8,128)(2,1)S(1)} %copy.26), channel_id=1, source_target_pairs={{0,8},{1,9},{2,10},{3,11},{4,12},{5,13},{6,14},{7,15},{16,24},{17,... | collective-permute-start | bytes 1572872 | tf_op jit(solution)/shard_map/ppermute | solution.py:31
  15.2 3.6 collective-permute-start.1
  18.8 2.2 collective-permute-start.2
  22.3 1.9 collective-permute-start.8
  25.7 56.6 %collective-permute-done.8 = s32[128]{0:T(128)S(1)} collective-permute-done((s32[128]{0:T(128)}, s32[128]{0:T(128)S(1)}, u32[]{:S(2)}, u32[]{:S(2)}) %collective-permute-start.8) | collective-permute-done | bytes 544 | tf_op jit(solution)/shard_map/ppermute | solution.py:31
  82.2 87.8 %collective-permute-start.9 = (s32[128]{0:T(128)}, s32[128]{0:T(128)S(1)}, u32[]{:S(2)}, u32[]{:S(2)}) collective-permute-start(s32[128]{0:T(128)} %param.10), channel_id=1, source_target_pairs={{0,7},{1,8},{2,9},{3,10},{4,11},{5,12},{6,13},{7,14},{8,15},{16,23... | collective-permute-start | bytes 1544 | tf_op jit(solution)/shard_map/ppermute | solution.py:31
  177.3 8.0 %collective-permute-start.12 = (s32[128]{0:T(128)}, s32[128]{0:T(128)S(1)}, u32[]{:S(2)}, u32[]{:S(2)}) collective-permute-start(s32[128]{0:T(128)} %param.10), channel_id=1, source_target_pairs={{0,4},{1,5},{2,6},{3,7},{4,8},{5,9},{6,10},{7,11},{8,12},{9,13},{1... | collective-permute-start | bytes 1544 | tf_op jit(solution)/shard_map/ppermute | solution.py:31
  186.7 3.1 collective-permute-start.13
  191.2 5.1 %collective-permute-start.14 = (s32[128]{0:T(128)}, s32[128]{0:T(128)S(1)}, u32[]{:S(2)}, u32[]{:S(2)}) collective-permute-start(s32[128]{0:T(128)} %param.10), channel_id=1, source_target_pairs={{0,2},{1,3},{2,4},{3,5},{4,6},{5,7},{6,8},{7,9},{8,10},{9,11},{10,... | collective-permute-start | bytes 1544 | tf_op jit(solution)/shard_map/ppermute | solution.py:31
  200.4 11.4 %collective-permute-start.4 = (bf16[128,2048]{0,1:T(8,128)(2,1)S(1)}, bf16[128,2048]{0,1:T(8,128)(2,1)S(1)}, u32[]{:S(2)}, u32[]{:S(2)}) collective-permute-start(bf16[128,2048]{0,1:T(8,128)(2,1)S(1)} %copy.26), channel_id=1, source_target_pairs={{0,4},{1,5},{2,6},{3,7},{4,8},{5,9},{6,10},{7,11},{8,12},{9,13},{1... | collective-permute-start | bytes 1572872 | tf_op jit(solution)/shard_map/ppermute | solution.py:31
  214.2 1.9 collective-permute-start.5
  216.3 2.2 collective-permute-start.6
  218.6 3.6 collective-permute-start.7
  222.6 2.7 collective-permute-done.5
  225.4 11.1 %collective-permute-done.6 = bf16[128,2048]{0,1:T(8,128)(2,1)S(1)} collective-permute-done((bf16[128,2048]{0,1:T(8,128)(2,1)S(1)}, bf16[128,2048]{0,1:T(8,128)(2,1)S(1)}, u32[]{:S(2)}, u32[]{:S(2)}) %collective-permute-start.6) | collective-permute-done | bytes 524320 | tf_op jit(solution)/shard_map/ppermute | solution.py:31
  236.9 1.9 fusion.32
  238.8 4.2 %fusion.33 = f32[8,2,128]{2,1,0:T(2,128)} fusion(pred[128,1152]{0,1:T(8,128)(4,1)S(1)} %compare_and_fusion, bf16[1152,8,128,1]{0,2,3,1:T(8,128)(2,1)S(1)} %bitcast.41, bf16[128,8,2,128]{3,2,1,0:T(2,128)(2,1)S(1)} %reshape.150), kind=kOutput, calls=%fused_computation.59 | convolution fusion | flops 613418112 | bytes 3039232 | tf_op jit(solution)/shard_map/sub | solution.py:81
  243.0 6.3 %fusion.6 = bf16[8,128,2,128]{3,1,2,0:T(8,128)(2,1)S(1)} fusion(bf16[1152,8,128,1]{0,2,3,1:T(8,128)(2,1)} %bitcast.43, f32[8,2,128]{2,1,0:T(2,128)} %fusion.33, pred[128,1152]{0,1:T(8,128)(4,1)S(1)} %compare_and_fusion, bf16[1152,8,128,1]{0,2,3,1:T(8,128)(2,1)S(1)} %bitcast.42, bf16[128,8,2,128]{3,2,1,0:T(2,128)(2,1)S(1)} %reshape.150), kind=kOutput, calls=%fused_computation.10 | convolution fusion | flops 1220021376 | bytes 5922816 | tf_op jit(solution)/shard_map/hgqk,khd->qhgd/dot_general | solution.py:83
  249.4 6.8 %fusion.36 = (bf16[128,2688]{1,0:T(8,128)(2,1)}, f32[128,2688]{1,0:T(8,128)S(1)}) fusion(bf16[128,2048]{0,1:T(8,128)(2,1)S(1)} %bitcast.45, bf16[2048,2688]{1,0:T(8,128)(2,1)} %all-gather.2.cloned.1.call-done, bf16[128,2688]{1,0:T(8,128)(2,1)} %param.11), kind=kOutput, calls=%fused_computation.60 | convolution fusion | flops 1410318336 | bytes 14286848 | tf_op jit(solution)/shard_map/dot_general | solution.py:88
  256.5 3.2 collective-permute-start.16
  262.4 4.8 %collective-permute-start.17 = (bf16[4,2688]{1,0:T(4,128)(2,1)S(1)}, bf16[4,2688]{1,0:T(4,128)(2,1)S(1)}, u32[]{:S(2)}, u32[]{:S(2)}) collective-permute-start(bf16[4,2688]{1,0:T(4,128)(2,1)S(1)} %collective-permute-done.16), channel_id=1, source_target_pairs={{0,1},{1,2},{2,3},{3,4},{4,5},{5,6},{6,7},{7,8},{8,9},{9,10},{10,1... | collective-permute-start | bytes 64520 | tf_op jit(solution)/shard_map/ppermute | solution.py:21
  268.3 5.4 %collective-permute-start.18 = (bf16[4,2688]{1,0:T(4,128)(2,1)S(1)}, bf16[4,2688]{1,0:T(4,128)(2,1)S(1)}, u32[]{:S(2)}, u32[]{:S(2)}) collective-permute-start(bf16[4,2688]{1,0:T(4,128)(2,1)S(1)} %collective-permute-done.17), channel_id=1, source_target_pairs={{0,1},{1,2},{2,3},{3,4},{4,5},{5,6},{6,7},{7,8},{8,9},{9,10},{10,1... | collective-permute-start | bytes 64520 | tf_op jit(solution)/shard_map/ppermute | solution.py:21
  274.6 3.4 collective-permute-start.19
  278.4 2.0 collective-permute-start.27
  282.5 3.8 collective-permute-start.28
  287.8 4.4 %collective-permute-start.29 = (bf16[4,2688]{1,0:T(4,128)(2,1)S(1)}, bf16[4,2688]{1,0:T(4,128)(2,1)S(1)}, u32[]{:S(2)}, u32[]{:S(2)}) collective-permute-start(bf16[4,2688]{1,0:T(4,128)(2,1)S(1)} %collective-permute-done.28), channel_id=1, source_target_pairs={{0,15},{1,0},{2,1},{3,2},{4,3},{5,4},{6,5},{7,6},{8,7},{9,8},{10,9... | collective-permute-start | bytes 64520 | tf_op jit(solution)/shard_map/ppermute | solution.py:23
  293.7 4.4 %collective-permute-start.30 = (bf16[4,2688]{1,0:T(4,128)(2,1)S(1)}, bf16[4,2688]{1,0:T(4,128)(2,1)S(1)}, u32[]{:S(2)}, u32[]{:S(2)}) collective-permute-start(bf16[4,2688]{1,0:T(4,128)(2,1)S(1)} %collective-permute-done.29), channel_id=1, source_target_pairs={{0,15},{1,0},{2,1},{3,2},{4,3},{5,4},{6,5},{7,6},{8,7},{9,8},{10,9... | collective-permute-start | bytes 64520 | tf_op jit(solution)/shard_map/ppermute | solution.py:23
  299.6 4.5 %collective-permute-done.23 = bf16[4,2688]{1,0:T(4,128)(2,1)S(1)} collective-permute-done((bf16[4,2688]{1,0:T(4,128)(2,1)S(1)}, bf16[4,2688]{1,0:T(4,128)(2,1)S(1)}, u32[]{:S(2)}, u32[]{:S(2)}) %collective-permute-start.23) | collective-permute-done | bytes 21536 | tf_op jit(solution)/shard_map/ppermute | solution.py:21
  304.9 4.4 %fusion.37 = (f32[64]{0:T(128)S(1)}, f32[64,1024]{1,0:T(8,128)S(1)}) fusion(bf16[1024,2688]{1,0:T(8,128)(2,1)} %param.14, bf16[128,2688]{1,0:T(8,128)(2,1)S(1)} %concatenate.14, s32[]{:T(128)S(6)} %select_n.23), kind=kOutput, calls=%fused_computation.61 | convolution fusion | flops 352387008 | bytes 6111492 | tf_op jit(solution)/shard_map/dot_general | solution.py:99
  309.4 29.5 %pmax.7 = f32[64]{0:T(128)S(1)} all-reduce(f32[64]{0:T(128)S(1)} %get-tuple-element.9), channel_id=1, replica_groups=mesh['parts'=2,'seq'=16] {'seq'}, use_global_device_ids=true, to_apply=%region_4.5 | all-reduce | flops 64 | bytes 512 | tf_op jit(solution)/shard_map/pmax | solution.py:105
  339.1 29.5 %psum.7 = f32[64]{0:T(128)S(1)} all-reduce(f32[64]{0:T(128)S(1)} %exponential_reduce_fusion), channel_id=1, replica_groups=mesh['parts'=2,'seq'=16] {'seq'}, use_global_device_ids=true, to_apply=%region_6.7 | all-reduce | flops 64 | bytes 512 | tf_op jit(solution)/shard_map/psum | solution.py:106
  369.5 29.5 %all-reduce = f32[64]{0:T(128)S(1)} all-reduce(f32[64]{0:T(128)S(1)} %get-tuple-element.3), channel_id=2, replica_groups=mesh['parts'=2,'seq'=16] {'seq'}, use_global_device_ids=true, to_apply=%region_8.9.clone | all-reduce | flops 64 | bytes 512
  (83 shorter events, 36.1 us)
Async XLA Ops:
  7.2 242.2 %all-gather.2.cloned.1.call-start = ((), (), s32[]{:S(2)}) async-start(), calls=%async_computation | async-start | bytes 11698176 | tf_op jit(solution)/shard_map/all_gather | solution.py:90
  9.2 205.0 %collective-permute-start = (bf16[128,2048]{0,1:T(8,128)(2,1)S(1)}, bf16[128,2048]{0,1:T(8,128)(2,1)S(1)}, u32[]{:S(2)}, u32[]{:S(2)}) collective-permute-start(bf16[128,2048]{0,1:T(8,128)(2,1)S(1)} %copy.26), channel_id=1, source_target_pairs={{0,8},{1,9},{2,10},{3,11},{4,12},{5,13},{6,14},{7,15},{16,24},{17,... | collective-permute-start | bytes 1572872 | tf_op jit(solution)/shard_map/ppermute | solution.py:31
  15.2 201.0 %collective-permute-start.1 = (bf16[128,2048]{0,1:T(8,128)(2,1)S(1)}, bf16[128,2048]{0,1:T(8,128)(2,1)S(1)}, u32[]{:S(2)}, u32[]{:S(2)}) collective-permute-start(bf16[128,2048]{0,1:T(8,128)(2,1)S(1)} %copy.26), channel_id=1, source_target_pairs={{0,7},{1,8},{2,9},{3,10},{4,11},{5,12},{6,13},{7,14},{8,15},{16,23... | collective-permute-start | bytes 1572872 | tf_op jit(solution)/shard_map/ppermute | solution.py:31
  18.8 199.8 %collective-permute-start.2 = (bf16[128,2048]{0,1:T(8,128)(2,1)S(1)}, bf16[128,2048]{0,1:T(8,128)(2,1)S(1)}, u32[]{:S(2)}, u32[]{:S(2)}) collective-permute-start(bf16[128,2048]{0,1:T(8,128)(2,1)S(1)} %copy.26), channel_id=1, source_target_pairs={{0,6},{1,7},{2,8},{3,9},{4,10},{5,11},{6,12},{7,13},{8,14},{9,15},... | collective-permute-start | bytes 1572872 | tf_op jit(solution)/shard_map/ppermute | solution.py:31
  21.0 201.3 %collective-permute-start.3 = (bf16[128,2048]{0,1:T(8,128)(2,1)S(1)}, bf16[128,2048]{0,1:T(8,128)(2,1)S(1)}, u32[]{:S(2)}, u32[]{:S(2)}) collective-permute-start(bf16[128,2048]{0,1:T(8,128)(2,1)S(1)} %copy.26), channel_id=1, source_target_pairs={{0,5},{1,6},{2,7},{3,8},{4,9},{5,10},{6,11},{7,12},{8,13},{9,14},{... | collective-permute-start | bytes 1572872 | tf_op jit(solution)/shard_map/ppermute | solution.py:31
  22.3 59.9 %collective-permute-start.8 = (s32[128]{0:T(128)}, s32[128]{0:T(128)S(1)}, u32[]{:S(2)}, u32[]{:S(2)}) collective-permute-start(s32[128]{0:T(128)} %param.10), channel_id=1, source_target_pairs={{0,8},{1,9},{2,10},{3,11},{4,12},{5,13},{6,14},{7,15},{16,24},{17,... | collective-permute-start | bytes 1544 | tf_op jit(solution)/shard_map/ppermute | solution.py:31
  82.2 89.3 %collective-permute-start.9 = (s32[128]{0:T(128)}, s32[128]{0:T(128)S(1)}, u32[]{:S(2)}, u32[]{:S(2)}) collective-permute-start(s32[128]{0:T(128)} %param.10), channel_id=1, source_target_pairs={{0,7},{1,8},{2,9},{3,10},{4,11},{5,12},{6,13},{7,14},{8,15},{16,23... | collective-permute-start | bytes 1544 | tf_op jit(solution)/shard_map/ppermute | solution.py:31
  171.5 3.1 collective-permute-start.10
  174.6 2.7 collective-permute-start.11
  177.3 9.5 %collective-permute-start.12 = (s32[128]{0:T(128)}, s32[128]{0:T(128)S(1)}, u32[]{:S(2)}, u32[]{:S(2)}) collective-permute-start(s32[128]{0:T(128)} %param.10), channel_id=1, source_target_pairs={{0,4},{1,5},{2,6},{3,7},{4,8},{5,9},{6,10},{7,11},{8,12},{9,13},{1... | collective-permute-start | bytes 1544 | tf_op jit(solution)/shard_map/ppermute | solution.py:31
  186.7 4.5 %collective-permute-start.13 = (s32[128]{0:T(128)}, s32[128]{0:T(128)S(1)}, u32[]{:S(2)}, u32[]{:S(2)}) collective-permute-start(s32[128]{0:T(128)} %param.10), channel_id=1, source_target_pairs={{0,3},{1,4},{2,5},{3,6},{4,7},{5,8},{6,9},{7,10},{8,11},{9,12},{10... | collective-permute-start | bytes 1544 | tf_op jit(solution)/shard_map/ppermute | solution.py:31
  191.2 6.6 %collective-permute-start.14 = (s32[128]{0:T(128)}, s32[128]{0:T(128)S(1)}, u32[]{:S(2)}, u32[]{:S(2)}) collective-permute-start(s32[128]{0:T(128)} %param.10), channel_id=1, source_target_pairs={{0,2},{1,3},{2,4},{3,5},{4,6},{5,7},{6,8},{7,9},{8,10},{9,11},{10,... | collective-permute-start | bytes 1544 | tf_op jit(solution)/shard_map/ppermute | solution.py:31
  197.8 2.6 collective-permute-start.15
  200.4 22.1 %collective-permute-start.4 = (bf16[128,2048]{0,1:T(8,128)(2,1)S(1)}, bf16[128,2048]{0,1:T(8,128)(2,1)S(1)}, u32[]{:S(2)}, u32[]{:S(2)}) collective-permute-start(bf16[128,2048]{0,1:T(8,128)(2,1)S(1)} %copy.26), channel_id=1, source_target_pairs={{0,4},{1,5},{2,6},{3,7},{4,8},{5,9},{6,10},{7,11},{8,12},{9,13},{1... | collective-permute-start | bytes 1572872 | tf_op jit(solution)/shard_map/ppermute | solution.py:31
  214.2 11.1 %collective-permute-start.5 = (bf16[128,2048]{0,1:T(8,128)(2,1)S(1)}, bf16[128,2048]{0,1:T(8,128)(2,1)S(1)}, u32[]{:S(2)}, u32[]{:S(2)}) collective-permute-start(bf16[128,2048]{0,1:T(8,128)(2,1)S(1)} %copy.26), channel_id=1, source_target_pairs={{0,3},{1,4},{2,5},{3,6},{4,7},{5,8},{6,9},{7,10},{8,11},{9,12},{10... | collective-permute-start | bytes 1572872 | tf_op jit(solution)/shard_map/ppermute | solution.py:31
  216.3 20.2 %collective-permute-start.6 = (bf16[128,2048]{0,1:T(8,128)(2,1)S(1)}, bf16[128,2048]{0,1:T(8,128)(2,1)S(1)}, u32[]{:S(2)}, u32[]{:S(2)}) collective-permute-start(bf16[128,2048]{0,1:T(8,128)(2,1)S(1)} %copy.26), channel_id=1, source_target_pairs={{0,2},{1,3},{2,4},{3,5},{4,6},{5,7},{6,8},{7,9},{8,10},{9,11},{10,... | collective-permute-start | bytes 1572872 | tf_op jit(solution)/shard_map/ppermute | solution.py:31
  218.6 18.0 %collective-permute-start.7 = (bf16[128,2048]{0,1:T(8,128)(2,1)S(1)}, bf16[128,2048]{0,1:T(8,128)(2,1)S(1)}, u32[]{:S(2)}, u32[]{:S(2)}) collective-permute-start(bf16[128,2048]{0,1:T(8,128)(2,1)S(1)} %copy.26), channel_id=1, source_target_pairs={{0,1},{1,2},{2,3},{3,4},{4,5},{5,6},{6,7},{7,8},{8,9},{9,10},{10,1... | collective-permute-start | bytes 1572872 | tf_op jit(solution)/shard_map/ppermute | solution.py:31
  256.5 6.0 %collective-permute-start.16 = (bf16[4,2688]{1,0:T(4,128)(2,1)S(1)}, bf16[4,2688]{1,0:T(4,128)(2,1)S(1)}, u32[]{:S(2)}, u32[]{:S(2)}) collective-permute-start(bf16[4,2688]{1,0:T(4,128)(2,1)S(1)} %fusion.23), channel_id=1, source_target_pairs={{0,1},{1,2},{2,3},{3,4},{4,5},{5,6},{6,7},{7,8},{8,9},{9,10},{10,1... | collective-permute-start | bytes 64520 | tf_op jit(solution)/shard_map/ppermute | solution.py:21
  259.6 7.6 %collective-permute-start.24 = (bf16[4,2688]{1,0:T(4,128)(2,1)S(1)}, bf16[4,2688]{1,0:T(4,128)(2,1)S(1)}, u32[]{:S(2)}, u32[]{:S(2)}) collective-permute-start(bf16[4,2688]{1,0:T(4,128)(2,1)S(1)} %fusion.23), channel_id=1, source_target_pairs={{0,15},{1,0},{2,1},{3,2},{4,3},{5,4},{6,5},{7,6},{8,7},{9,8},{10,9... | collective-permute-start | bytes 64520 | tf_op jit(solution)/shard_map/ppermute | solution.py:23
  262.4 5.9 %collective-permute-start.17 = (bf16[4,2688]{1,0:T(4,128)(2,1)S(1)}, bf16[4,2688]{1,0:T(4,128)(2,1)S(1)}, u32[]{:S(2)}, u32[]{:S(2)}) collective-permute-start(bf16[4,2688]{1,0:T(4,128)(2,1)S(1)} %collective-permute-done.16), channel_id=1, source_target_pairs={{0,1},{1,2},{2,3},{3,4},{4,5},{5,6},{6,7},{7,8},{8,9},{9,10},{10,1... | collective-permute-start | bytes 64520 | tf_op jit(solution)/shard_map/ppermute | solution.py:21
  267.2 7.2 %collective-permute-start.25 = (bf16[4,2688]{1,0:T(4,128)(2,1)S(1)}, bf16[4,2688]{1,0:T(4,128)(2,1)S(1)}, u32[]{:S(2)}, u32[]{:S(2)}) collective-permute-start(bf16[4,2688]{1,0:T(4,128)(2,1)S(1)} %collective-permute-done.24), channel_id=1, source_target_pairs={{0,15},{1,0},{2,1},{3,2},{4,3},{5,4},{6,5},{7,6},{8,7},{9,8},{10,9... | collective-permute-start | bytes 64520 | tf_op jit(solution)/shard_map/ppermute | solution.py:23
  268.3 6.2 %collective-permute-start.18 = (bf16[4,2688]{1,0:T(4,128)(2,1)S(1)}, bf16[4,2688]{1,0:T(4,128)(2,1)S(1)}, u32[]{:S(2)}, u32[]{:S(2)}) collective-permute-start(bf16[4,2688]{1,0:T(4,128)(2,1)S(1)} %collective-permute-done.17), channel_id=1, source_target_pairs={{0,1},{1,2},{2,3},{3,4},{4,5},{5,6},{6,7},{7,8},{8,9},{9,10},{10,1... | collective-permute-start | bytes 64520 | tf_op jit(solution)/shard_map/ppermute | solution.py:21
  274.4 4.0 collective-permute-start.26
  274.6 5.9 %collective-permute-start.19 = (bf16[4,2688]{1,0:T(4,128)(2,1)S(1)}, bf16[4,2688]{1,0:T(4,128)(2,1)S(1)}, u32[]{:S(2)}, u32[]{:S(2)}) collective-permute-start(bf16[4,2688]{1,0:T(4,128)(2,1)S(1)} %collective-permute-done.18), channel_id=1, source_target_pairs={{0,1},{1,2},{2,3},{3,4},{4,5},{5,6},{6,7},{7,8},{8,9},{9,10},{10,1... | collective-permute-start | bytes 64520 | tf_op jit(solution)/shard_map/ppermute | solution.py:21
  278.4 4.1 %collective-permute-start.27 = (bf16[4,2688]{1,0:T(4,128)(2,1)S(1)}, bf16[4,2688]{1,0:T(4,128)(2,1)S(1)}, u32[]{:S(2)}, u32[]{:S(2)}) collective-permute-start(bf16[4,2688]{1,0:T(4,128)(2,1)S(1)} %collective-permute-done.26), channel_id=1, source_target_pairs={{0,15},{1,0},{2,1},{3,2},{4,3},{5,4},{6,5},{7,6},{8,7},{9,8},{10,9... | collective-permute-start | bytes 64520 | tf_op jit(solution)/shard_map/ppermute | solution.py:23
  280.5 5.9 %collective-permute-start.20 = (bf16[4,2688]{1,0:T(4,128)(2,1)S(1)}, bf16[4,2688]{1,0:T(4,128)(2,1)S(1)}, u32[]{:S(2)}, u32[]{:S(2)}) collective-permute-start(bf16[4,2688]{1,0:T(4,128)(2,1)S(1)} %collective-permute-done.19), channel_id=1, source_target_pairs={{0,1},{1,2},{2,3},{3,4},{4,5},{5,6},{6,7},{7,8},{8,9},{9,10},{10,1... | collective-permute-start | bytes 64520 | tf_op jit(solution)/shard_map/ppermute | solution.py:21
  282.5 5.3 %collective-permute-start.28 = (bf16[4,2688]{1,0:T(4,128)(2,1)S(1)}, bf16[4,2688]{1,0:T(4,128)(2,1)S(1)}, u32[]{:S(2)}, u32[]{:S(2)}) collective-permute-start(bf16[4,2688]{1,0:T(4,128)(2,1)S(1)} %collective-permute-done.27), channel_id=1, source_target_pairs={{0,15},{1,0},{2,1},{3,2},{4,3},{5,4},{6,5},{7,6},{8,7},{9,8},{10,9... | collective-permute-start | bytes 64520 | tf_op jit(solution)/shard_map/ppermute | solution.py:23
  286.4 5.9 %collective-permute-start.21 = (bf16[4,2688]{1,0:T(4,128)(2,1)S(1)}, bf16[4,2688]{1,0:T(4,128)(2,1)S(1)}, u32[]{:S(2)}, u32[]{:S(2)}) collective-permute-start(bf16[4,2688]{1,0:T(4,128)(2,1)S(1)} %collective-permute-done.20), channel_id=1, source_target_pairs={{0,1},{1,2},{2,3},{3,4},{4,5},{5,6},{6,7},{7,8},{8,9},{9,10},{10,1... | collective-permute-start | bytes 64520 | tf_op jit(solution)/shard_map/ppermute | solution.py:21
  287.8 5.9 %collective-permute-start.29 = (bf16[4,2688]{1,0:T(4,128)(2,1)S(1)}, bf16[4,2688]{1,0:T(4,128)(2,1)S(1)}, u32[]{:S(2)}, u32[]{:S(2)}) collective-permute-start(bf16[4,2688]{1,0:T(4,128)(2,1)S(1)} %collective-permute-done.28), channel_id=1, source_target_pairs={{0,15},{1,0},{2,1},{3,2},{4,3},{5,4},{6,5},{7,6},{8,7},{9,8},{10,9... | collective-permute-start | bytes 64520 | tf_op jit(solution)/shard_map/ppermute | solution.py:23
  292.3 5.9 %collective-permute-start.22 = (bf16[4,2688]{1,0:T(4,128)(2,1)S(1)}, bf16[4,2688]{1,0:T(4,128)(2,1)S(1)}, u32[]{:S(2)}, u32[]{:S(2)}) collective-permute-start(bf16[4,2688]{1,0:T(4,128)(2,1)S(1)} %collective-permute-done.21), channel_id=1, source_target_pairs={{0,1},{1,2},{2,3},{3,4},{4,5},{5,6},{6,7},{7,8},{8,9},{9,10},{10,1... | collective-permute-start | bytes 64520 | tf_op jit(solution)/shard_map/ppermute | solution.py:21
  293.7 5.9 %collective-permute-start.30 = (bf16[4,2688]{1,0:T(4,128)(2,1)S(1)}, bf16[4,2688]{1,0:T(4,128)(2,1)S(1)}, u32[]{:S(2)}, u32[]{:S(2)}) collective-permute-start(bf16[4,2688]{1,0:T(4,128)(2,1)S(1)} %collective-permute-done.29), channel_id=1, source_target_pairs={{0,15},{1,0},{2,1},{3,2},{4,3},{5,4},{6,5},{7,6},{8,7},{9,8},{10,9... | collective-permute-start | bytes 64520 | tf_op jit(solution)/shard_map/ppermute | solution.py:23
  298.2 5.9 %collective-permute-start.23 = (bf16[4,2688]{1,0:T(4,128)(2,1)S(1)}, bf16[4,2688]{1,0:T(4,128)(2,1)S(1)}, u32[]{:S(2)}, u32[]{:S(2)}) collective-permute-start(bf16[4,2688]{1,0:T(4,128)(2,1)S(1)} %collective-permute-done.22), channel_id=1, source_target_pairs={{0,1},{1,2},{2,3},{3,4},{4,5},{5,6},{6,7},{7,8},{8,9},{9,10},{10,1... | collective-permute-start | bytes 64520 | tf_op jit(solution)/shard_map/ppermute | solution.py:21
  (3 other events, 104.8 us)
Sparse Core Ops, SparseCore 0:
  10.3 136.2 all-gather.1
